TPU v7x, 256 devices: a whole 4x4x8 slice. The times are simulated.
256 devices in a mesh: dict: 16 (over x, z_hi, core), tensor: 16 (over z_lo, y).
Axes of the slice: x: 4, y: 4, z: 8 (z_hi: 2, z_lo: 4; z = z_hi * 4 + z_lo), core: 2. Of those that a mesh axis runs over, the one named last changes fastest.
Arguments:
- residual: bfloat16 [4096, 8192], P('dict', 'tensor'), may hold values from -10 to 10
- norm_gain: float32 [8192], replicated, may hold values from 0.1 to 1.9
- w_query: bfloat16 [8192, 8192], P('dict', 'tensor'), may hold values from -2 to 2
- w_key: bfloat16 [8192, 1024], P('dict'), may hold values from -2 to 2
- value_weight: bfloat16 [8192, 1024], P('dict'), may hold values from -0.0625 to 0.0625
- w_out: bfloat16 [8192, 8192], P('tensor', 'dict'), may hold values from -0.0625 to 0.0625
- decoder: bfloat16 [131072, 8192], P('dict', 'tensor'), may hold values from -0.5 to 0.5
- block_ids: int32 [2], replicated, may hold values from 0 to 1023, as said below
- latent_ids: int32 [4096, 64], P('dict'), may hold values from 0 to 131071, as said below
- latent_vals: float32 [4096, 64], P('dict'), may hold values from 0.5 to 4
- prompt_lens: int32 [16], P('dict'), may hold values from 32 to 256, as said below
Outputs:
- ablations: bfloat16 [2, 4096, 8192], P(None, 'dict', 'tensor')
Inputs may be any that keep to these rules, and one draw needn't show every extreme that they name: `block_ids`: 2 distinct blocks, one of them the last block; block b covers latents b * 128 to b * 128 + 127. `latent_ids`: about half of a row's entries name latents of the swept blocks; a row may name a latent more than once. Prompt p uses its first prompt_lens[p] rows; some prompt uses all 256 and some only 32.
All inputs are finite; a program needn't handle non-finite values.
Results may differ from a plain program's by a relative error of at most 0.009.
Values may be sent and summed in bfloat16 or wider, within the bound.
No kernel may reach another device: no remote copies, remote signals or barrier semaphores. Data moves between devices by JAX's collectives and lax.ppermute only.
A program may use at most 192 MiB of HBM per device.

v0:
```python
import math
import jax
import jax.numpy as jnp
from jax import lax
from jax.sharding import PartitionSpec as P

QUERY_HEADS = 64
KEY_VALUE_HEADS = 8
HEAD_SIZE = 128
BLOCK = 128
PROMPT_ROWS = 256
ABLATION_STEPS = 2
ROPE_BASE = 1000000.0
EPSILON = 1e-06
MASKED = -1e30


def rope_tables(length, head_dim):
    frequency = ROPE_BASE ** (-(jnp.arange(head_dim // 2, dtype=jnp.float32) * 2.0) / head_dim)
    angles = jnp.arange(length, dtype=jnp.float32)[:, None] * frequency[None, :]
    angles = jnp.concatenate([angles, angles], axis=-1)
    return (jnp.cos(angles), jnp.sin(angles))


def apply_rotary(feature_map, cosine_table, sine_table):
    half_width = feature_map.shape[-1] // 2
    first_half = feature_map[..., :half_width]
    second_half = feature_map[..., half_width:]
    turned = jnp.concatenate([-second_half, first_half], axis=-1)
    return feature_map * cosine_table + turned * sine_table


def dense_codes(latent_ids, latent_vals, first_latent):
    offsets = latent_ids - first_latent
    columns = jnp.arange(BLOCK, dtype=jnp.int32)
    matched = offsets[:, :, None] == columns[None, None, :]
    picked = jnp.where(matched, latent_vals[:, :, None], jnp.zeros((), jnp.float32))
    return jnp.sum(picked, axis=1).astype(jnp.bfloat16)


def owner_rows(decoder, block_num):
    lat_count = decoder.shape[0]
    first_latent = block_num * BLOCK
    owner_dict = first_latent // lat_count
    row_offset = first_latent - owner_dict * lat_count
    return (lax.dynamic_slice_in_dim(decoder, row_offset, BLOCK, 0), owner_dict)


DICT = ("dict_x", "dict_z", "core")
DICT_RING = ("dict_z", "core", "dict_x")


def dict_index():
    return (
        lax.axis_index("dict_x") * lax.axis_size("dict_z") + lax.axis_index("dict_z")
    ) * lax.axis_size("core") + lax.axis_index("core")


def dict_size():
    return lax.axis_size("dict_x") * lax.axis_size("dict_z") * lax.axis_size("core")


def butterfly_sum(value, axis, count):
    step = 1
    while step < count:
        pairs = [(i, i ^ step) for i in range(count)]
        value = value + lax.ppermute(value, axis, pairs)
        step *= 2
    return value


def fetch_blocks(decoder, block_ids):
    dict_pos = dict_index()
    dict_count = dict_size()
    blocks = []
    for number in range(ABLATION_STEPS):
        dec_rows, owner_dict = owner_rows(decoder, block_ids[number])
        blocks.append(jnp.where(dict_pos == owner_dict, dec_rows, jnp.zeros_like(dec_rows)))
    held = jnp.stack(blocks)
    step = 1
    while step < dict_count:
        pairs = [(i, i ^ step) for i in range(dict_count)]
        held = held + lax.ppermute(held, DICT, pairs)
        step *= 2
    return held


def body(
    residual,
    norm_gain,
    w_query,
    w_key,
    value_weight,
    w_out,
    decoder,
    block_ids,
    latent_ids,
    latent_vals,
    prompt_lens,
):
    row_count = residual.shape[0]
    col_count = residual.shape[1]
    tensor_pos = lax.axis_index("tensor")
    tensor_count = lax.axis_size("tensor")
    full_width = col_count * tensor_count
    head_cols = w_query.shape[1]
    heads_dev = head_cols // HEAD_SIZE
    query_group_size = QUERY_HEADS // KEY_VALUE_HEADS
    kv_index = tensor_pos * heads_dev // query_group_size
    assert 2 * heads_dev <= query_group_size
    is_key_side = tensor_pos % 2 == 0
    key_cols = lax.dynamic_slice_in_dim(w_key, kv_index * HEAD_SIZE, HEAD_SIZE, 1)
    value_cols = lax.dynamic_slice_in_dim(value_weight, kv_index * HEAD_SIZE, HEAD_SIZE, 1)
    kv_cols = jnp.where(is_key_side, key_cols, value_cols)
    packed = jnp.concatenate([w_query, kv_cols, w_out.T], axis=1)
    ring_gathered = lax.all_gather(packed, DICT_RING, axis=0, tiled=True)
    coef_list = [
        dense_codes(latent_ids, latent_vals, block_ids[number] * BLOCK)
        for number in range(ABLATION_STEPS)
    ]
    col_list = []
    dec_blocks = fetch_blocks(decoder, block_ids)
    for number in range(ABLATION_STEPS):
        dec_slice = dec_blocks[number]
        removed = jnp.dot(coef_list[number], dec_slice, preferred_element_type=jnp.float32)
        col_list.append((residual.astype(jnp.float32) - removed).astype(jnp.bfloat16))
    own_cols = jnp.stack(col_list)
    widened = own_cols.astype(jnp.float32)
    sum_sq = butterfly_sum(
        jnp.sum(widened * widened, axis=-1, keepdims=True), "tensor", tensor_count
    )
    mean_sq = sum_sq / full_width
    gain_cols = lax.dynamic_slice_in_dim(norm_gain, tensor_pos * col_count, col_count)
    normed_cols = (widened * lax.rsqrt(mean_sq + EPSILON) * gain_cols).astype(jnp.bfloat16)
    normed_cols, ring_gathered = lax.optimization_barrier((normed_cols, ring_gathered))
    x_count = lax.axis_size("dict_x")
    z_count = lax.axis_size("dict_z")
    core_count = lax.axis_size("core")
    gathered = ring_gathered.reshape((z_count, core_count, x_count) + packed.shape)
    gathered = jnp.transpose(gathered, (2, 0, 1, 3, 4)).reshape(-1, packed.shape[1])
    normed = lax.all_gather(normed_cols, "tensor", axis=2, tiled=True)
    normed = normed.reshape(ABLATION_STEPS * row_count, full_width)
    qkv_cols = head_cols + HEAD_SIZE
    qkv = jnp.dot(normed, gathered[:, :qkv_cols], preferred_element_type=jnp.float32)
    query_vec = qkv[:, :head_cols]
    kv_vector = qkv[:, head_cols:qkv_cols]
    prompt_count = row_count // PROMPT_ROWS
    cosine_table, sine_table = rope_tables(PROMPT_ROWS, HEAD_SIZE)
    query_vec = apply_rotary(
        query_vec.reshape(ABLATION_STEPS, prompt_count, PROMPT_ROWS, heads_dev, HEAD_SIZE),
        cosine_table[:, None, :],
        sine_table[:, None, :],
    ).astype(jnp.bfloat16)
    kv_vector = kv_vector.reshape(ABLATION_STEPS, prompt_count, PROMPT_ROWS, HEAD_SIZE)
    kv_rotated = apply_rotary(kv_vector, cosine_table, sine_table)
    own_kv = jnp.where(is_key_side, kv_rotated, kv_vector).astype(jnp.bfloat16)
    tensor_pairs = [(i, i ^ 1) for i in range(tensor_count)]
    other_kv = lax.ppermute(own_kv, "tensor", tensor_pairs)
    key_vector = jnp.where(is_key_side, own_kv, other_kv)
    value_vector = jnp.where(is_key_side, other_kv, own_kv)
    positions = jnp.arange(PROMPT_ROWS, dtype=jnp.int32)
    scores = jnp.einsum(
        "spqhd,spkd->sphqk", query_vec, key_vector, preferred_element_type=jnp.float32
    ) / math.sqrt(HEAD_SIZE)
    allowed = (positions[None, None, :] <= positions[None, :, None]) & (
        positions[None, None, :] < prompt_lens[:, None, None]
    )
    scores = jnp.where(allowed[None, :, None, :, :], scores, MASKED)
    weights = jax.nn.softmax(scores, axis=-1).astype(jnp.bfloat16)
    context = jnp.einsum(
        "sphqk,spkd->spqhd", weights, value_vector, preferred_element_type=jnp.float32
    )
    context = context.astype(jnp.bfloat16).reshape(ABLATION_STEPS * row_count, head_cols)
    partial_value = lax.dot_general(
        context,
        gathered[:, qkv_cols:],
        (((1,), (1,)), ((), ())),
        preferred_element_type=jnp.float32,
    ).astype(jnp.bfloat16)
    summed = lax.psum_scatter(
        partial_value.astype(jnp.float32).astype(jnp.bfloat16),
        "tensor",
        scatter_dimension=1,
        tiled=True,
    ).astype(jnp.float32)
    result = own_cols.reshape(ABLATION_STEPS * row_count, col_count).astype(jnp.float32) + summed
    return result.astype(jnp.bfloat16).reshape(ABLATION_STEPS, row_count, col_count)


def solution(mesh):
    dict_count = mesh.shape["dict"]
    core_count = 2 if dict_count % 2 == 0 else 1
    z_count = 2 if dict_count % (2 * core_count) == 0 else 1
    x_count = dict_count // (core_count * z_count)
    devices = mesh.devices.reshape(x_count, z_count, core_count, mesh.shape["tensor"])
    fine = jax.sharding.Mesh(devices, ("dict_x", "dict_z", "core", "tensor"))
    in_specs = (
        P(DICT, "tensor"),
        P(),
        P(DICT, "tensor"),
        P(DICT, None),
        P(DICT, None),
        P("tensor", DICT),
        P(DICT, "tensor"),
        P(),
        P(DICT, None),
        P(DICT, None),
        P(DICT),
    )
    out_specs = P(None, DICT, "tensor")
    return jax.shard_map(body, mesh=fine, in_specs=in_specs, out_specs=out_specs, check_vma=False)
```

profile of v0, /device:TPU:6, one launch (start us, length us, event | category | flops | bytes accessed | tf_op | source)
XLA Modules:
  0.0 456.7 jit_solution(7599784094827931474)
XLA Ops:
  6.5 1.3 copy.67
  8.8 2.2 pad_maximum_fusion
  14.2 1.5 collective-permute-done
  15.8 7.3 %collective-permute-start.1 = (bf16[2,128,512]{2,1,0:T(8,128)(2,1)S(1)}, bf16[2,128,512]{2,1,0:T(8,128)(2,1)S(1)}, u32[]{:S(2)}, u32[]{:S(2)}) collective-permute-start(bf16[2,128,512]{2,1,0:T(8,128)(2,1)S(1)} %fusion.34), channel_id=1, source_target_pairs={{0,32},{16,48},{32,0},{48,16},{64,96},{80,112},{96,64},{112,80},{1... | collective-permute-start | bytes 786440 | tf_op jit(solution)/shard_map/ppermute | solution.py:83
  23.1 16.6 %collective-permute-done.1 = bf16[2,128,512]{2,1,0:T(8,128)(2,1)S(1)} collective-permute-done((bf16[2,128,512]{2,1,0:T(8,128)(2,1)S(1)}, bf16[2,128,512]{2,1,0:T(8,128)(2,1)S(1)}, u32[]{:S(2)}, u32[]{:S(2)}) %collective-permute-start.1) | collective-permute-done | bytes 262176 | tf_op jit(solution)/shard_map/ppermute | solution.py:83
  41.0 8.9 %collective-permute-done.2 = bf16[2,128,512]{2,1,0:T(8,128)(2,1)S(1)} collective-permute-done((bf16[2,128,512]{2,1,0:T(8,128)(2,1)S(1)}, bf16[2,128,512]{2,1,0:T(8,128)(2,1)S(1)}, u32[]{:S(2)}, u32[]{:S(2)}) %collective-permute-start.2) | collective-permute-done | bytes 262176 | tf_op jit(solution)/shard_map/ppermute | solution.py:83
  50.1 7.8 %select_reduce_fusion.1 = (bf16[256,128]{1,0:T(8,128)(2,1)S(1)}, bf16[256,128]{1,0:T(8,128)(2,1)S(1)}) fusion(f32[256,64]{1,0:T(8,128)S(1)} %copy.65, s32[256,64]{1,0:T(8,128)S(1)} %copy.64, s32[256,64]{1,0:T(8,128)S(1)} %copy.66), kind=kLoop, calls=%fused_computation.6 | loop fusion | flops 12517376 | bytes 327680 | tf_op jit(solution)/shard_map/reduce_sum | solution.py:38
  58.6 2.2 collective-permute-start.4
  60.9 1.6 collective-permute-done.4
  62.4 3.5 collective-permute-start.5
  66.0 1.6 collective-permute-done.5
  67.5 4.9 %collective-permute-start.6 = (f32[2,256,1]{1,0,2:T(2,128)S(1)}, f32[2,256,1]{1,0,2:T(2,128)S(1)}, u32[]{:S(2)}, u32[]{:S(2)}) collective-permute-start(f32[2,256,1]{1,0,2:T(2,128)S(1)} %add.88), channel_id=1, source_target_pairs={{0,4},{1,5},{2,6},{3,7},{4,0},{5,1},{6,2},{7,3},{8,12},{9,13},{10,... | collective-permute-start | bytes 6152 | tf_op jit(solution)/shard_map/ppermute | solution.py:67
  72.4 1.6 collective-permute-done.6
  74.0 3.1 collective-permute-start.7
  79.6 129.5 %all-gather.3.cloned.1.call-done = bf16[8192,1152]{1,0:T(8,128)(2,1)} async-done(((bf16[512,1152]{1,0:T(8,128)(2,1)}), bf16[8192,1152]{1,0:T(8,128)(2,1)}) %all-gather.3.cloned.1.call-update) | async-done | bytes 18874384 | tf_op jit(solution)/shard_map/all_gather | solution.py:116
  210.8 16.8 %copy.68 = bf16[4,2,2,512,1152]{4,3,2,1,0:T(8,128)(2,1)} copy(bf16[4,2,2,512,1152]{4,3,0,2,1:T(8,128)(2,1)} %bitcast.73) | data formatting | bytes 37748736 | tf_op jit(solution)/shard_map/transpose | solution.py:140
  227.6 81.7 %all-gather.5.cloned.1.call-done = bf16[2,256,8192]{2,1,0:T(8,128)(2,1)} async-done(((bf16[2,256,512]{2,1,0:T(8,128)(2,1)}), bf16[2,256,8192]{2,1,0:T(8,128)(2,1)}) %all-gather.5.cloned.1.call-update) | async-done | bytes 8388624 | tf_op jit(solution)/shard_map/all_gather | solution.py:141
  309.3 14.5 %fusion = f32[512,640]{1,0:T(8,128)S(1)} fusion(bf16[512,8192]{1,0:T(8,128)(2,1)} %bitcast.80, bf16[8192,1152]{1,0:T(8,128)(2,1)} %bitcast.74), kind=kOutput, calls=%fused_computation.1 | convolution fusion | flops 5368709120 | bytes 20185088 | tf_op jit(solution)/shard_map/dot_general | solution.py:144
  325.5 1.6 copy_bitcast_fusion
  327.5 2.1 collective-permute-done.8
  329.6 2.4 fusion.37
  333.2 10.2 %convolution_convert_fusion = bf16[512,8192]{1,0:T(8,128)(2,1)} fusion(bf16[8192,1152]{1,0:T(8,128)(2,1)} %bitcast.75, bf16[64,8,4,128]{3,2,1,0:T(4,128)(2,1)S(1)} %bitcast.78), kind=kOutput, calls=%fused_computation | convolution fusion | flops 4299161600 | bytes 17301504 | tf_op jit(solution)/shard_map/dot_general | solution.py:174
  343.5 104.7 %reduce-scatter.2.cloned.1.call-done = bf16[512,512]{1,0:T(8,128)(2,1)} async-done(((bf16[512,8192]{1,0:T(8,128)(2,1)}), bf16[512,512]{1,0:T(8,128)(2,1)}) %reduce-scatter.2.cloned.1.call-update) | async-done | bytes 524304 | tf_op jit(solution)/shard_map/reduce_scatter | solution.py:180
  448.1 2.0 fusion.13
  (60 shorter events, 11.7 us)
Async XLA Ops:
  6.5 202.6 %all-gather.3.cloned.1.call-start = ((), (), s32[]{:S(2)}) async-start(), calls=%async_computation.1 | async-start | bytes 20054016 | tf_op jit(solution)/shard_map/all_gather | solution.py:116
  6.5 4.5 copy-start.3
  11.0 29.7 %copy-start.1 = (s32[256,64]{0,1:T(8,128)S(1)}, s32[256,64]{0,1:T(8,128)}, u32[]{:S(2)}) copy-start(s32[256,64]{0,1:T(8,128)} %param.19) | copy-start | bytes 196612
  11.0 29.9 %copy-start.2 = (f32[256,64]{0,1:T(8,128)S(1)}, f32[256,64]{0,1:T(8,128)}, u32[]{:S(2)}) copy-start(f32[256,64]{0,1:T(8,128)} %param.20) | copy-start | bytes 196612
  11.0 298.3 %all-gather.5.cloned.1.call-start = ((), (), s32[]{:S(2)}) async-start(), calls=%async_computation.2 | async-start | bytes 8912896 | tf_op jit(solution)/shard_map/all_gather | solution.py:141
  14.1 43.9 %copy-start = (bf16[256,512]{1,0:T(8,128)(2,1)S(1)}, bf16[256,512]{1,0:T(8,128)(2,1)}, u32[]{:S(2)}) copy-start(bf16[256,512]{1,0:T(8,128)(2,1)} %param.11) | copy-start | bytes 786436
  14.1 1.6 collective-permute-start
  15.8 23.9 %collective-permute-start.1 = (bf16[2,128,512]{2,1,0:T(8,128)(2,1)S(1)}, bf16[2,128,512]{2,1,0:T(8,128)(2,1)S(1)}, u32[]{:S(2)}, u32[]{:S(2)}) collective-permute-start(bf16[2,128,512]{2,1,0:T(8,128)(2,1)S(1)} %fusion.34), channel_id=1, source_target_pairs={{0,32},{16,48},{32,0},{48,16},{64,96},{80,112},{96,64},{112,80},{1... | collective-permute-start | bytes 786440 | tf_op jit(solution)/shard_map/ppermute | solution.py:83
  39.7 10.2 %collective-permute-start.2 = (bf16[2,128,512]{2,1,0:T(8,128)(2,1)S(1)}, bf16[2,128,512]{2,1,0:T(8,128)(2,1)S(1)}, u32[]{:S(2)}, u32[]{:S(2)}) collective-permute-start(bf16[2,128,512]{2,1,0:T(8,128)(2,1)S(1)} %fusion.41), channel_id=1, source_target_pairs={{0,64},{16,80},{32,96},{48,112},{64,0},{80,16},{96,32},{112,48},{1... | collective-permute-start | bytes 786440 | tf_op jit(solution)/shard_map/ppermute | solution.py:83
  50.0 8.0 %collective-permute-start.3 = (bf16[2,128,512]{2,1,0:T(8,128)(2,1)S(1)}, bf16[2,128,512]{2,1,0:T(8,128)(2,1)S(1)}, u32[]{:S(2)}, u32[]{:S(2)}) collective-permute-start(bf16[2,128,512]{2,1,0:T(8,128)(2,1)S(1)} %add.84), channel_id=1, source_target_pairs={{0,128},{16,144},{32,160},{48,176},{64,192},{80,208},{96,224},{112... | collective-permute-start | bytes 786440 | tf_op jit(solution)/shard_map/ppermute | solution.py:83
  58.6 3.8 collective-permute-start.4
  62.4 5.1 %collective-permute-start.5 = (f32[2,256,1]{1,0,2:T(2,128)S(1)}, f32[2,256,1]{1,0,2:T(2,128)S(1)}, u32[]{:S(2)}, u32[]{:S(2)}) collective-permute-start(f32[2,256,1]{1,0,2:T(2,128)S(1)} %bitcast_add_fusion.1), channel_id=1, source_target_pairs={{0,2},{1,3},{2,0},{3,1},{4,6},{5,7},{6,4},{7,5},{8,10},{9,11},{10,... | collective-permute-start | bytes 6152 | tf_op jit(solution)/shard_map/ppermute | solution.py:67
  67.5 6.5 %collective-permute-start.6 = (f32[2,256,1]{1,0,2:T(2,128)S(1)}, f32[2,256,1]{1,0,2:T(2,128)S(1)}, u32[]{:S(2)}, u32[]{:S(2)}) collective-permute-start(f32[2,256,1]{1,0,2:T(2,128)S(1)} %add.88), channel_id=1, source_target_pairs={{0,4},{1,5},{2,6},{3,7},{4,0},{5,1},{6,2},{7,3},{8,12},{9,13},{10,... | collective-permute-start | bytes 6152 | tf_op jit(solution)/shard_map/ppermute | solution.py:67
  74.0 4.6 %collective-permute-start.7 = (f32[2,256,1]{1,0,2:T(2,128)S(1)}, f32[2,256,1]{1,0,2:T(2,128)S(1)}, u32[]{:S(2)}, u32[]{:S(2)}) collective-permute-start(f32[2,256,1]{1,0,2:T(2,128)S(1)} %add.89), channel_id=1, source_target_pairs={{0,8},{1,9},{2,10},{3,11},{4,12},{5,13},{6,14},{7,15},{8,0},{9,1},... | collective-permute-start | bytes 6152 | tf_op jit(solution)/shard_map/ppermute | solution.py:67
  209.2 238.9 %reduce-scatter.2.cloned.1.call-start = ((), (), s32[]{:S(2)}) async-start(), calls=%async_computation.3 | async-start | bytes 8912896 | tf_op jit(solution)/shard_map/reduce_scatter | solution.py:180
  324.3 5.3 %collective-permute-start.8 = (bf16[2,1,256,128]{2,3,0,1:T(8,128)(2,1)S(1)}, bf16[2,1,256,128]{2,3,0,1:T(8,128)(2,1)S(1)}, u32[]{:S(2)}, u32[]{:S(2)}) collective-permute-start(bf16[2,1,256,128]{2,3,0,1:T(8,128)(2,1)S(1)} %fusion.21), channel_id=1, source_target_pairs={{0,1},{1,0},{2,3},{3,2},{4,5},{5,4},{6,7},{7,6},{8,9},{9,8},{10,11... | collective-permute-start | bytes 393224 | tf_op jit(solution)/shard_map/ppermute | solution.py:158
Sparse Core Ops, SparseCore 0:
  11.1 197.9 all-gather.2
  210.9 98.3 all-gather.4
  343.5 104.5 reduce-scatter.1
where the time goes:
time: 457 us
  waiting for transfers between devices  351 us (77%)
  matrix products  28.1 us (6%)
  starting transfers between devices  22.5 us (5%)
  local copies, waits for them, and re-layouts  21.8 us (5%)
  other arithmetic  18.2 us (4%)
  between operations  15.4 us (3%)
    all_gather x1, waiting for transfers between devices, body(): ring_gathered = lax.all_gather(packed, DICT_RING, axis=0, tiled=True)  130 us
    reduce_scatter x1, waiting for transfers between devices, body(): lax.psum_scatter(partial_value.astype(jnp.float32).astype(jnp.bfloat16),...  105 us
    all_gather x1, waiting for transfers between devices, body(): normed = lax.all_gather(normed_cols, 'tensor', axis=2, tiled=True)  81.7 us
    ppermute x4, waiting for transfers between devices, fetch_blocks(): held = held + lax.ppermute(held, DICT, pairs)  27 us
    transpose x1, local copies, waits for them, and re-layouts, body(): jnp.transpose(gathered, (2, 0, 1, 3, 4)).reshape(-1, packed.shape[1])  16.8 us
    dot_general x1, matrix products, body(): jnp.dot(normed, gathered[:, :qkv_cols], preferred_element_type=jnp.float32)  14.5 us
    ppermute x4, starting transfers between devices, butterfly_sum(): value = value + lax.ppermute(value, axis, pairs)  13.7 us
    dot_general x1, matrix products, body(): lax.dot_general(context, gathered[:, qkv_cols:], (((1,), (1,)), ((), ()))...  10.2 us
  transfers between devices with their start and end apart: 12, of which 11 were waited for; matrix products, arithmetic and copies ran while one was open for 7% of the time, Pallas kernels for 0%

commit v1 on v0

--- a/solution.py
+++ b/solution.py
@@ -113,7 +113,9 @@
     value_cols = lax.dynamic_slice_in_dim(value_weight, kv_index * HEAD_SIZE, HEAD_SIZE, 1)
     kv_cols = jnp.where(is_key_side, key_cols, value_cols)
     packed = jnp.concatenate([w_query, kv_cols, w_out.T], axis=1)
-    ring_gathered = lax.all_gather(packed, DICT_RING, axis=0, tiled=True)
+    ring_gathered = jnp.concatenate(
+        lax.all_to_all(jnp.stack([packed] * lax.axis_size(DICT_RING)), DICT_RING, 0, 0), axis=0
+    )
     coef_list = [
         dense_codes(latent_ids, latent_vals, block_ids[number] * BLOCK)
         for number in range(ABLATION_STEPS)

time: 457 us -> 737 us (1.61)
  waiting for transfers between devices: 351 us -> 617 us
  local copies, waits for them, and re-layouts: 21.8 us -> 35.3 us
    ppermute x4, waiting for transfers between devices: 27 us -> 422 us  [fetch_blocks(): held = held + lax.ppermute(held, DICT, pairs)]
    all_gather x1 -> x0, waiting for transfers between devices: 130 us -> none  [body(): ring_gathered = lax.all_gather(packed, DICT_RING, axis=0, tiled=True)]
    all_to_all x0 -> x1, starting transfers between devices: none -> 11.5 us  [body(): lax.all_to_all(jnp.stack([packed] * lax.axis_size(DICT_RING)), DICT_RING,...]
    ppermute x4, starting transfers between devices: 13.7 us -> 5.66 us  [butterfly_sum(): value = value + lax.ppermute(value, axis, pairs)]
  transfers between devices with their start and end apart: 12 -> 12, of which waited for: 11 -> 10; matrix products, arithmetic and copies ran while one was open for 7% -> 5% of each run, Pallas kernels for 0% -> 0%
where the time goes in v1:
time: 737 us
  waiting for transfers between devices  617 us (84%)
  local copies, waits for them, and re-layouts  35.3 us (5%)
  matrix products  28.5 us (4%)
  starting transfers between devices  25.7 us (3%)
  between operations  15.7 us (2%)
  other arithmetic  14.2 us (2%)
    ppermute x4, waiting for transfers between devices, fetch_blocks(): held = held + lax.ppermute(held, DICT, pairs)  422 us
    reduce_scatter x1, waiting for transfers between devices, body(): lax.psum_scatter(partial_value.astype(jnp.float32).astype(jnp.bfloat16),...  104 us
    all_gather x1, waiting for transfers between devices, body(): normed = lax.all_gather(normed_cols, 'tensor', axis=2, tiled=True)  80.2 us
    transpose x1, local copies, waits for them, and re-layouts, body(): jnp.transpose(gathered, (2, 0, 1, 3, 4)).reshape(-1, packed.shape[1])  16.9 us
  transfers between devices with their start and end apart: 12, of which 10 were waited for; matrix products, arithmetic and copies ran while one was open for 5% of the time, Pallas kernels for 0%

profile of v1, /device:TPU:6, one launch (start us, length us, event | category | flops | bytes accessed | tf_op | source)
XLA Modules:
  0.0 736.8 jit_solution(7227208808920055129)
XLA Ops:
  9.9 7.0 stack.20
  16.9 11.5 %all-to-all-start = ((bf16[16,512,1152]{2,1,0:T(8,128)(2,1)}), bf16[16,512,1152]{2,1,0:T(8,128)(2,1)}, u32[]{:S(2)}, u32[]{:S(2)}) async-start(bf16[16,512,1152]{2,1,0:T(8,128)(2,1)} %stack.20), calls=%async_computation | async-start | bytes 37748736 | tf_op jit(solution)/shard_map/all_to_all | solution.py:117
  31.7 1.4 collective-permute-done
  33.1 5.5 collective-permute-start.1
  38.6 413.8 %collective-permute-done.1 = bf16[2,128,512]{2,1,0:T(8,128)(2,1)S(1)} collective-permute-done((bf16[2,128,512]{2,1,0:T(8,128)(2,1)S(1)}, bf16[2,128,512]{2,1,0:T(8,128)(2,1)S(1)}, u32[]{:S(2)}, u32[]{:S(2)}) %collective-permute-start.1) | collective-permute-done | bytes 262176 | tf_op jit(solution)/shard_map/ppermute | solution.py:83
  453.7 6.6 collective-permute-done.2
  460.4 1.6 collective-permute-start.3
  461.9 7.8 %select_reduce_fusion.1 = (bf16[256,128]{1,0:T(8,128)(2,1)S(1)}, bf16[256,128]{1,0:T(8,128)(2,1)S(1)}) fusion(f32[256,64]{1,0:T(8,128)S(1)} %copy.70, s32[256,64]{1,0:T(8,128)S(1)} %copy.69, s32[256,64]{1,0:T(8,128)S(1)} %copy.71), kind=kLoop, calls=%fused_computation.6 | loop fusion | flops 12517376 | bytes 327680 | tf_op jit(solution)/shard_map/reduce_sum | solution.py:38
  470.5 1.7 collective-permute-start.4
  472.1 2.0 collective-permute-done.4
  474.1 3.2 collective-permute-start.5
  477.3 1.9 collective-permute-done.5
  479.2 3.6 collective-permute-done.6
  484.4 2.9 collective-permute-done.7
  491.8 16.9 %copy.76 = bf16[4,2,2,512,1152]{4,3,2,1,0:T(8,128)(2,1)} copy(bf16[4,2,2,512,1152]{4,3,0,2,1:T(8,128)(2,1)} %bitcast.15) | data formatting | bytes 37748736 | tf_op jit(solution)/shard_map/transpose | solution.py:142
  508.7 80.2 %all-gather.2.cloned.1.call-done = bf16[2,256,8192]{2,1,0:T(8,128)(2,1)} async-done(((bf16[2,256,512]{2,1,0:T(8,128)(2,1)}), bf16[2,256,8192]{2,1,0:T(8,128)(2,1)}) %all-gather.2.cloned.1.call-update) | async-done | bytes 8388624 | tf_op jit(solution)/shard_map/all_gather | solution.py:143
  588.9 14.5 %fusion = f32[512,640]{1,0:T(8,128)S(1)} fusion(bf16[512,8192]{1,0:T(8,128)(2,1)} %bitcast.82, bf16[8192,1152]{1,0:T(8,128)(2,1)} %bitcast.75), kind=kOutput, calls=%fused_computation.1 | convolution fusion | flops 5368709120 | bytes 20185088 | tf_op jit(solution)/shard_map/dot_general | solution.py:146
  604.5 1.6 fusion.35
  607.8 1.4 collective-permute-done.8
  609.3 1.9 fusion.37
  611.5 1.5 fusion.4
  613.2 10.2 %convolution_convert_fusion = bf16[512,8192]{1,0:T(8,128)(2,1)} fusion(bf16[8192,1152]{1,0:T(8,128)(2,1)} %bitcast.76, bf16[64,8,4,128]{3,2,1,0:T(4,128)(2,1)S(1)} %bitcast.79), kind=kOutput, calls=%fused_computation | convolution fusion | flops 4299161600 | bytes 17301504 | tf_op jit(solution)/shard_map/dot_general | solution.py:176
  624.4 103.5 %reduce-scatter.2.cloned.1.call-done = bf16[512,512]{1,0:T(8,128)(2,1)} async-done(((bf16[512,8192]{1,0:T(8,128)(2,1)}), bf16[512,512]{1,0:T(8,128)(2,1)}) %reduce-scatter.2.cloned.1.call-update) | async-done | bytes 524304 | tf_op jit(solution)/shard_map/reduce_scatter | solution.py:182
  727.9 2.0 fusion.13
  (71 shorter events, 17.0 us)
Async XLA Ops:
  6.5 2.6 copy-start.3
  16.9 11.6 %copy-start.6 = (s32[2]{0:T(128)S(1)}, s32[2]{0:T(128)}, u32[]{:S(2)}) copy-start(s32[2]{0:T(128)} %param.18) | copy-start | bytes 28
  16.9 471.4 %all-to-all-start = ((bf16[16,512,1152]{2,1,0:T(8,128)(2,1)}), bf16[16,512,1152]{2,1,0:T(8,128)(2,1)}, u32[]{:S(2)}, u32[]{:S(2)}) async-start(bf16[16,512,1152]{2,1,0:T(8,128)(2,1)} %stack.20), calls=%async_computation | async-start | bytes 37748736 | tf_op jit(solution)/shard_map/all_to_all | solution.py:117
  28.5 424.9 %copy-start.4 = (s32[256,64]{0,1:T(8,128)S(1)}, s32[256,64]{0,1:T(8,128)}, u32[]{:S(2)}) copy-start(s32[256,64]{0,1:T(8,128)} %param.19) | copy-start | bytes 196612
  28.5 425.1 %copy-start.5 = (f32[256,64]{0,1:T(8,128)S(1)}, f32[256,64]{0,1:T(8,128)}, u32[]{:S(2)}) copy-start(f32[256,64]{0,1:T(8,128)} %param.20) | copy-start | bytes 196612
  28.5 560.4 %all-gather.2.cloned.1.call-start = ((), (), s32[]{:S(2)}) async-start(), calls=%async_computation.2 | async-start | bytes 8912896 | tf_op jit(solution)/shard_map/all_gather | solution.py:143
  31.5 438.4 %copy-start.2 = (bf16[256,512]{1,0:T(8,128)(2,1)S(1)}, bf16[256,512]{1,0:T(8,128)(2,1)}, u32[]{:S(2)}) copy-start(bf16[256,512]{1,0:T(8,128)(2,1)} %param.11) | copy-start | bytes 786436
  31.5 1.6 collective-permute-start
  33.1 419.2 %collective-permute-start.1 = (bf16[2,128,512]{2,1,0:T(8,128)(2,1)S(1)}, bf16[2,128,512]{2,1,0:T(8,128)(2,1)S(1)}, u32[]{:S(2)}, u32[]{:S(2)}) collective-permute-start(bf16[2,128,512]{2,1,0:T(8,128)(2,1)S(1)} %fusion.34), channel_id=1, source_target_pairs={{0,32},{16,48},{32,0},{48,16},{64,96},{80,112},{96,64},{112,80},{1... | collective-permute-start | bytes 786440 | tf_op jit(solution)/shard_map/ppermute | solution.py:83
  452.4 7.9 %collective-permute-start.2 = (bf16[2,128,512]{2,1,0:T(8,128)(2,1)S(1)}, bf16[2,128,512]{2,1,0:T(8,128)(2,1)S(1)}, u32[]{:S(2)}, u32[]{:S(2)}) collective-permute-start(bf16[2,128,512]{2,1,0:T(8,128)(2,1)S(1)} %fusion.41), channel_id=1, source_target_pairs={{0,64},{16,80},{32,96},{48,112},{64,0},{80,16},{96,32},{112,48},{1... | collective-permute-start | bytes 786440 | tf_op jit(solution)/shard_map/ppermute | solution.py:83
  460.4 9.4 %collective-permute-start.3 = (bf16[2,128,512]{2,1,0:T(8,128)(2,1)S(1)}, bf16[2,128,512]{2,1,0:T(8,128)(2,1)S(1)}, u32[]{:S(2)}, u32[]{:S(2)}) collective-permute-start(bf16[2,128,512]{2,1,0:T(8,128)(2,1)S(1)} %add.84), channel_id=1, source_target_pairs={{0,128},{16,144},{32,160},{48,176},{64,192},{80,208},{96,224},{112... | collective-permute-start | bytes 786440 | tf_op jit(solution)/shard_map/ppermute | solution.py:83
  470.3 38.4 %copy-start = (bf16[1,256,512]{2,1,0:T(8,128)(2,1)}, bf16[1,256,512]{2,1,0:T(8,128)(2,1)S(1)}, u32[]{:S(2)}) copy-start(bf16[1,256,512]{2,1,0:T(8,128)(2,1)S(1)} %fusion.7) | copy-start | bytes 786436
  470.5 3.7 collective-permute-start.4
  474.1 5.1 collective-permute-start.5
  479.2 3.6 collective-permute-start.6
  482.8 4.5 collective-permute-start.7
  488.3 239.6 %reduce-scatter.2.cloned.1.call-start = ((), (), s32[]{:S(2)}) async-start(), calls=%async_computation.3 | async-start | bytes 8912896 | tf_op jit(solution)/shard_map/reduce_scatter | solution.py:182
  603.8 5.4 collective-permute-start.8
  623.4 0.9 copy-start.1
Sparse Core Ops, SparseCore 0:
  488.4 100.3 all-gather.1
  623.5 104.3 reduce-scatter.1
